TPU v7x, 32 devices: a whole 2x2x4 slice. The times are simulated.
32 devices in a mesh: groups: 2 (over x), wide: 16 (over z, y, core).
Axes of the slice: x: 2, y: 2, z: 4, core: 2. Of those that a mesh axis runs over, the one named last changes fastest.
Arguments:
- query_act: bfloat16 [4096, 2048], P(('groups', 'wide')), parts along dimension 0, may hold values from -6 to 6
- query_grad: bfloat16 [4096, 4096], P(('groups', 'wide')), parts along dimension 0, may hold values from -6 to 6
- query_positions: int32 [4096], P(('groups', 'wide')), parts along dimension 0, may hold values from 0 to 4095
- act_basis: bfloat16 [2048, 1024], P(None, 'wide'), may hold values from -0.125 to 0.125
- grad_basis: bfloat16 [4096, 2048], P(None, 'wide'), may hold values from -0.09375 to 0.09375
- eig_values: bfloat16 [1024, 2048], P('wide'), may hold values from 0.05 to 50, as said below
- damping_index: int32 [12], P('groups'), parts along dimension 0, may hold values from 0 to 8
- train_act_rot: bfloat16 [1024, 6144], P(None, 'wide'), may hold values from -6 to 6
- train_grad_rot: bfloat16 [2048, 6144], P(None, 'wide'), may hold values from -6 to 6
- train_positions: int32 [6144], P('wide'), may hold values from 0 to 4095
Outputs:
- influences: float32 [12, 6144], P('groups', 'wide'), parts along dimension 0
There are 2 independent parts, one for each index of `groups`. A program takes and returns all parts, laid end to end along the dimension named above; an argument that names none is the same for every part. Nothing has to cross between parts.
Inputs may be any that keep to these rules, and one draw needn't show every extreme that they name: `eig_values`: positive corrected eigenvalues.
All inputs are finite; a program needn't handle non-finite values.
Results may differ from a plain program's by a relative error of at most 0.0059.
Values may be sent and summed in bfloat16 or wider, within the bound.
No kernel may reach another device: no remote copies, remote signals or barrier semaphores. Data moves between devices by JAX's collectives and lax.ppermute only.
A program may use at most 128 MiB of HBM per device.

v0:
```python
import math
import jax
import jax.numpy as jnp
from jax import lax
from jax.sharding import PartitionSpec as P

EIG_IN = 1024
EIG_OUT = 2048
PROMPT = 1024


def score_rows(grad_rows, eig_rows, dampings, train_act_rot, train_grad_rot):
    acts_rows = train_act_rot.astype(jnp.float32)
    grad_wide = grad_rows.astype(jnp.float32)
    eig_wide = eig_rows.astype(jnp.float32)
    results = []
    for damping in range(dampings.shape[0]):
        precond = (grad_wide / (eig_wide + dampings[damping])).astype(jnp.bfloat16)
        projected = jnp.dot(precond, train_grad_rot, preferred_element_type=jnp.float32)
        results.append(jnp.sum(projected * acts_rows, axis=0))
    return jnp.stack(results)


def shards(
    query_act,
    query_grad,
    query_positions,
    act_basis,
    grad_basis,
    eig_values,
    damping_index,
    train_act_rot,
    train_grad_rot,
    train_positions,
):
    act_full = jnp.dot(
        query_act,
        lax.all_gather(act_basis, "wide", axis=1, tiled=True),
        preferred_element_type=jnp.float32,
    )
    grad_full = jnp.dot(
        query_grad,
        lax.all_gather(grad_basis, "wide", axis=1, tiled=True),
        preferred_element_type=jnp.float32,
    )
    act_rot = act_full.astype(jnp.bfloat16)
    grad_rot = grad_full.astype(jnp.bfloat16)
    query_weight = jnp.where(query_positions >= PROMPT, 1.0, 0.0).astype(jnp.bfloat16)
    grad_kept = grad_rot * query_weight[:, None]
    eig_total = lax.psum(jnp.sum(eig_values.astype(jnp.float32)), "wide")
    mean_eig = eig_total / (EIG_IN * EIG_OUT)
    dampings = mean_eig * jnp.exp2(damping_index.astype(jnp.float32) - 4.0)
    partial_whole = lax.dot_general(
        act_rot, grad_kept, (((0,), (0,)), ((), ())), preferred_element_type=jnp.float32
    )
    query_gradient = lax.psum(partial_whole, "wide").astype(jnp.bfloat16)
    totals = score_rows(
        query_gradient,
        lax.all_gather(eig_values, "wide", axis=0, tiled=True),
        dampings,
        train_act_rot,
        train_grad_rot,
    )
    query_count = query_act.shape[0] * lax.axis_size("wide")
    factor = mean_eig * (1.0 / math.sqrt(float(query_count) * EIG_IN * EIG_OUT))
    train_weight = jnp.where(train_positions >= PROMPT, 1.0, 0.0).astype(jnp.float32)
    return totals * factor * train_weight[None, :]


def solution(mesh):
    in_specs = (
        P(("groups", "wide"), None),
        P(("groups", "wide"), None),
        P(("groups", "wide")),
        P(None, "wide"),
        P(None, "wide"),
        P("wide", None),
        P("groups"),
        P(None, "wide"),
        P(None, "wide"),
        P("wide"),
    )
    out_specs = P("groups", "wide")
    return jax.shard_map(shards, mesh=mesh, in_specs=in_specs, out_specs=out_specs, check_vma=False)
```

profile of v0, /device:TPU:1, one launch (start us, length us, event | category | flops | bytes accessed | tf_op | source)
XLA Modules:
  0.0 428.8 jit_solution(4725387925321449047)
XLA Ops:
  6.5 0.0 copy-start
  6.5 0.0 all-gather.6.cloned.1.call-start
  6.5 0.7 all-gather.6.cloned.1.call-update
  7.3 0.0 all-gather.4.cloned.1.call-start
  7.3 0.7 all-gather.4.cloned.1.call-update
  8.0 0.0 all-gather.8.cloned.1.call-start
  8.1 0.7 all-gather.8.cloned.1.call-update
  8.7 1.7 convert_reduce_fusion
  10.4 0.7 fusion.38
  11.1 0.7 compare_select_fusion
  11.8 0.0 copy-start.1
  11.8 130.6 %all-gather.6.cloned.1.call-done = bf16[4096,2048]{1,0:T(8,128)(2,1)} async-done(((bf16[4096,128]{1,0:T(8,128)(2,1)}), bf16[4096,2048]{1,0:T(8,128)(2,1)}) %all-gather.6.cloned.1.call-update) | async-done | bytes 16777232 | tf_op jit(solution)/shard_map/all_gather | solution.py:43
  142.4 8.4 %fusion.18 = bf16[128,2048]{1,0:T(8,128)(2,1)S(1)} fusion(bf16[128,4096]{1,0:T(8,128)(2,1)} %param.11, bf16[4096,2048]{1,0:T(8,128)(2,1)} %all-gather.6.cloned.1.call-done, bf16[128]{0:T(256)(128)(2,1)S(1)} %fusion.38), kind=kOutput, calls=%fused_computation.31 | convolution fusion | flops 2148007936 | bytes 18350336 | tf_op jit(solution)/shard_map/dot_general | solution.py:41
  150.8 42.5 %all-gather.4.cloned.1.call-done = bf16[2048,1024]{0,1:T(8,128)(2,1)} async-done(((bf16[2048,64]{0,1:T(8,128)(2,1)}), bf16[2048,1024]{0,1:T(8,128)(2,1)}) %all-gather.4.cloned.1.call-update) | async-done | bytes 4194320 | tf_op jit(solution)/shard_map/all_gather | solution.py:38
  193.3 0.0 copy-done.1
  193.3 8.1 %fusion.37 = f32[1024,2048]{1,0:T(8,128)} fusion(bf16[128,2048]{1,0:T(8,128)(2,1)S(1)} %fusion.18, bf16[128,2048]{1,0:T(8,128)(2,1)S(1)} %copy-done.1, bf16[2048,1024]{0,1:T(8,128)(2,1)} %all-gather.4.cloned.1.call-done), kind=kOutput, calls=%fused_computation.39 | convolution fusion | flops 1073872896 | bytes 13631488 | tf_op jit(solution)/shard_map/dot_general | solution.py:53
  201.4 0.0 copy-start.5
  201.4 0.0 copy-start.4
  201.4 195.6 %all-reduce.2 = (bf16[1024,2048]{1,0:T(8,128)(2,1)}, f32[]{:T(128)}) all-reduce(f32[1024,2048]{1,0:T(8,128)} %fusion.37, f32[]{:T(128)} %convert_reduce_fusion), channel_id=1, replica_groups=mesh['groups'=2,'wide'=16] {'wide'}, use_global_device_ids=true, to_apply=%region_0.1 | all-reduce | flops 2097153 | bytes 12582920 | tf_op jit(solution)/shard_map/psum | solution.py:56
  397.7 0.0 copy-done.5
  397.8 0.7 fusion.39
  398.4 0.0 all-gather.8.cloned.1.call-done
  398.4 0.0 copy-done
  398.4 0.0 copy-done.4
  398.4 0.0 copy-start.2
  398.4 0.0 copy-start.3
  398.5 7.0 %fusion.24 = f32[384]{0:T(512)S(1)} fusion(bf16[1024,384]{1,0:T(8,128)(2,1)S(1)} %copy-done.4, bf16[2048,384]{1,0:T(8,128)(2,1)S(1)} %copy-done, bf16[1024,2048]{1,0:T(8,128)(2,1)} %get-tuple-element.5, bf16[1024,2048]{1,0:T(8,128)(2,1)} %all-gather.8.cloned.1.call-done, f32[]{:T(128)} %bitcast.5), kind=kOutput, calls=%fused_computation.37 | convolution fusion | flops 1622277760 | bytes 10749444 | tf_op jit(solution)/shard_map/dot_general | solution.py:19
  405.5 0.0 copy-done.2
  405.5 0.0 copy-done.3
  405.5 3.0 fusion.23
  408.5 3.1 fusion.22
  411.6 3.0 fusion.21
  414.6 3.3 fusion.20
  417.9 3.0 fusion.19
  421.6 0.6 multiply_multiply_fusion
  (8 shorter events, 0.1 us)
Async XLA Ops:
  6.5 391.9 %copy-start = (bf16[2048,384]{1,0:T(8,128)(2,1)S(1)}, bf16[2048,384]{1,0:T(8,128)(2,1)}, u32[]{:S(2)}) copy-start(bf16[2048,384]{1,0:T(8,128)(2,1)} %param.18) | copy-start | bytes 4718596
  6.5 135.9 %all-gather.6.cloned.1.call-start = ((), (), s32[]{:S(2)}) async-start(), calls=%async_computation.1 | async-start | bytes 17825792 | tf_op jit(solution)/shard_map/all_gather | solution.py:43
  7.3 186.1 %all-gather.4.cloned.1.call-start = ((), (), s32[]{:S(2)}) async-start(), calls=%async_computation | async-start | bytes 4456448 | tf_op jit(solution)/shard_map/all_gather | solution.py:38
  8.0 390.4 %all-gather.8.cloned.1.call-start = ((), (), s32[]{:S(2)}) async-start(), calls=%async_computation.2 | async-start | bytes 4456448 | tf_op jit(solution)/shard_map/all_gather | solution.py:59
  11.8 181.6 %copy-start.1 = (bf16[128,2048]{1,0:T(8,128)(2,1)S(1)}, bf16[128,2048]{1,0:T(8,128)(2,1)}, u32[]{:S(2)}) copy-start(bf16[128,2048]{1,0:T(8,128)(2,1)} %param.10) | copy-start | bytes 1572868
  201.4 196.3 %copy-start.5 = (s32[6]{0:T(128)S(1)}, s32[6]{0:T(128)}, u32[]{:S(2)}) copy-start(s32[6]{0:T(128)} %param.16) | copy-start | bytes 76
  201.4 197.0 %copy-start.4 = (bf16[1024,384]{1,0:T(8,128)(2,1)S(1)}, bf16[1024,384]{1,0:T(8,128)(2,1)}, u32[]{:S(2)}) copy-start(bf16[1024,384]{1,0:T(8,128)(2,1)} %param.17) | copy-start | bytes 2359300
  398.4 7.0 %copy-start.2 = (bf16[1024,2048]{1,0:T(8,128)(2,1)S(1)}, bf16[1024,2048]{1,0:T(8,128)(2,1)}, u32[]{:S(2)}) copy-start(bf16[1024,2048]{1,0:T(8,128)(2,1)} %all-gather.8.cloned.1.call-done) | copy-start | bytes 12582916
  398.4 7.0 %copy-start.3 = (bf16[1024,2048]{1,0:T(8,128)(2,1)S(1)}, bf16[1024,2048]{1,0:T(8,128)(2,1)}, u32[]{:S(2)}) copy-start(bf16[1024,2048]{1,0:T(8,128)(2,1)} %get-tuple-element.5) | copy-start | bytes 12582916
Sparse Core Ops, SparseCore 0:
  9.5 132.8 all-gather.5
  144.6 48.7 all-gather.3
  195.5 67.8 all-gather.7
where the time goes:
time: 429 us
  blocking collectives  196 us (46%)
  waiting for transfers between devices  175 us (41%)
  matrix products  39 us (9%)
  between operations  14.5 us (3%)
    psum x1, blocking collectives, shards(): query_gradient = lax.psum(partial_whole, 'wide').astype(jnp.bfloat16)  196 us
    all_gather x1, waiting for transfers between devices, shards(): lax.all_gather(grad_basis, 'wide', axis=1, tiled=True)  131 us
    all_gather x1, waiting for transfers between devices, shards(): lax.all_gather(act_basis, 'wide', axis=1, tiled=True)  42.5 us
    dot_general x6, matrix products, score_rows(): jnp.dot(precond, train_grad_rot, preferred_element_type=jnp.float32)  22.4 us
  transfers between devices with their start and end apart: 3, of which 2 were waited for; matrix products, arithmetic and copies ran while one was open for 5% of the time, Pallas kernels for 0%

commit v1 on v0

--- a/solution.py
+++ b/solution.py
@@ -7,6 +7,23 @@
 EIG_IN = 1024
 EIG_OUT = 2048
 PROMPT = 1024
+
+
+def laid_out(tiles, dim):
+    tiles = jnp.moveaxis(tiles, 0, dim)
+    shape = tiles.shape
+    return tiles.reshape(*shape[:dim], shape[dim] * shape[dim + 1], *shape[dim + 2 :])
+
+
+def gather_around(x, axis, dim):
+    peers = lax.axis_size(axis)
+    ahead = [(i, (i + 1) % peers) for i in range(peers)]
+    blocks = [x]
+    while len(blocks) < peers:
+        blocks.append(lax.ppermute(blocks[-1], axis, ahead))
+    index = lax.axis_index(axis)
+    blocks = jnp.stack(blocks)[(index - jnp.arange(peers)) % peers]
+    return laid_out(blocks, dim)
 
 
 def score_rows(grad_rows, eig_rows, dampings, train_act_rot, train_grad_rot):
@@ -34,9 +51,7 @@
     train_positions,
 ):
     act_full = jnp.dot(
-        query_act,
-        lax.all_gather(act_basis, "wide", axis=1, tiled=True),
-        preferred_element_type=jnp.float32,
+        query_act, gather_around(act_basis, "wide", 1), preferred_element_type=jnp.float32
     )
     grad_full = jnp.dot(
         query_grad,

time: 429 us -> 430 us (level)
  waiting for transfers between devices: 175 us -> 148 us
  local copies, waits for them, and re-layouts: 0.75 us -> 18.3 us
  starting transfers between devices: 0.08 us -> 8.93 us
    ppermute x0 -> x15, waiting for transfers between devices: none -> 148 us  [gather_around(): blocks.append(lax.ppermute(blocks[-1], axis, ahead))]
    all_gather x1, waiting for transfers between devices: 131 us -> 0.01 us  [shards(): lax.all_gather(grad_basis, 'wide', axis=1, tiled=True)]
    all_gather x1 -> x0, waiting for transfers between devices: 42.5 us -> none  [shards(): lax.all_gather(act_basis, 'wide', axis=1, tiled=True)]
    unnamed x12 -> x27, local copies, waits for them, and re-layouts: 0.02 us -> 11.8 us
    ppermute x0 -> x15, starting transfers between devices: none -> 8.89 us  [gather_around(): blocks.append(lax.ppermute(blocks[-1], axis, ahead))]
    gather x0 -> x1, local copies, waits for them, and re-layouts: none -> 5.07 us  [gather_around(): blocks = jnp.stack(blocks)[(index - jnp.arange(peers)) % peers]]
  transfers between devices with their start and end apart: 3 -> 17, of which waited for: 2 -> 14; matrix products, arithmetic and copies ran while one was open for 5% -> 9% of each run, Pallas kernels for 0% -> 0%
where the time goes in v1:
time: 430 us; the launch traced here: 429 us
  blocking collectives  195 us (45%)
  waiting for transfers between devices  148 us (34%)
  matrix products  40 us (9%)
  local copies, waits for them, and re-layouts  18.3 us (4%)
  between operations  14.9 us (3%)
  starting transfers between devices  8.93 us (2%)
    psum x1, blocking collectives, shards(): query_gradient = lax.psum(partial_whole, 'wide').astype(jnp.bfloat16)  195 us
    ppermute x15, waiting for transfers between devices, gather_around(): blocks.append(lax.ppermute(blocks[-1], axis, ahead))  148 us
    dot_general x6, matrix products, score_rows(): jnp.dot(precond, train_grad_rot, preferred_element_type=jnp.float32)  21.9 us
    unnamed x27, local copies, waits for them, and re-layouts  11.8 us
    dot_general x1, matrix products, shards(): lax.dot_general(act_rot, grad_kept, (((0,), (0,)), ((), ())), preferred_e...  9.87 us
    ppermute x15, starting transfers between devices, gather_around(): blocks.append(lax.ppermute(blocks[-1], axis, ahead))  8.89 us
  transfers between devices with their start and end apart: 17, of which 14 were waited for; matrix products, arithmetic and copies ran while one was open for 9% of the time, Pallas kernels for 0%

profile of v1, /device:TPU:1, one launch (start us, length us, event | category | flops | bytes accessed | tf_op | source)
XLA Modules:
  0.0 428.8 jit_solution(15096294378719245484)
XLA Ops:
  6.5 0.7 all-gather.3.cloned.1.call-update
  7.3 0.0 all-gather.5.cloned.1.call-start
  7.3 2.7 collective-permute-start
  10.0 0.0 all-gather.5.cloned.1.call-update
  10.0 1.7 bitcast_dynamic-update-slice_fusion.15
  11.7 1.7 convert_reduce_fusion
  13.4 0.7 fusion.38
  14.1 0.7 compare_select_fusion.3
  14.8 0.0 collective-permute-done
  14.8 1.2 collective-permute-start.1
  16.0 0.7 bitcast_dynamic-update-slice_fusion.14
  16.7 2.6 collective-permute-done.1
  19.3 2.5 collective-permute-start.2
  21.8 0.7 bitcast_dynamic-update-slice_fusion.13
  22.5 8.1 %collective-permute-done.2 = bf16[2048,64]{0,1:T(8,128)(2,1)S(1)} collective-permute-done((bf16[2048,64]{0,1:T(8,128)(2,1)S(1)}, bf16[2048,64]{0,1:T(8,128)(2,1)S(1)}, u32[]{:S(2)}, u32[]{:S(2)}) %collective-permute-start.2) | collective-permute-done | bytes 262176 | tf_op jit(solution)/shard_map/ppermute | solution.py:23
  30.6 2.5 collective-permute-start.3
  33.1 0.7 bitcast_dynamic-update-slice_fusion.12
  33.8 7.1 %collective-permute-done.3 = bf16[2048,64]{0,1:T(8,128)(2,1)S(1)} collective-permute-done((bf16[2048,64]{0,1:T(8,128)(2,1)S(1)}, bf16[2048,64]{0,1:T(8,128)(2,1)S(1)}, u32[]{:S(2)}, u32[]{:S(2)}) %collective-permute-start.3) | collective-permute-done | bytes 262176 | tf_op jit(solution)/shard_map/ppermute | solution.py:23
  40.9 0.0 collective-permute-start.4
  40.9 0.7 bitcast_dynamic-update-slice_fusion.11
  41.6 13.4 %collective-permute-done.4 = bf16[2048,64]{0,1:T(8,128)(2,1)S(1)} collective-permute-done((bf16[2048,64]{0,1:T(8,128)(2,1)S(1)}, bf16[2048,64]{0,1:T(8,128)(2,1)S(1)}, u32[]{:S(2)}, u32[]{:S(2)}) %collective-permute-start.4) | collective-permute-done | bytes 262176 | tf_op jit(solution)/shard_map/ppermute | solution.py:23
  55.0 0.0 collective-permute-start.5
  55.0 0.7 bitcast_dynamic-update-slice_fusion.10
  55.7 13.1 %collective-permute-done.5 = bf16[2048,64]{0,1:T(8,128)(2,1)S(1)} collective-permute-done((bf16[2048,64]{0,1:T(8,128)(2,1)S(1)}, bf16[2048,64]{0,1:T(8,128)(2,1)S(1)}, u32[]{:S(2)}, u32[]{:S(2)}) %collective-permute-start.5) | collective-permute-done | bytes 262176 | tf_op jit(solution)/shard_map/ppermute | solution.py:23
  68.8 0.0 collective-permute-start.6
  68.8 0.7 bitcast_dynamic-update-slice_fusion.9
  69.6 8.1 %collective-permute-done.6 = bf16[2048,64]{0,1:T(8,128)(2,1)S(1)} collective-permute-done((bf16[2048,64]{0,1:T(8,128)(2,1)S(1)}, bf16[2048,64]{0,1:T(8,128)(2,1)S(1)}, u32[]{:S(2)}, u32[]{:S(2)}) %collective-permute-start.6) | collective-permute-done | bytes 262176 | tf_op jit(solution)/shard_map/ppermute | solution.py:23
  77.7 0.0 collective-permute-start.7
  77.7 0.7 bitcast_dynamic-update-slice_fusion.8
  78.4 13.1 %collective-permute-done.7 = bf16[2048,64]{0,1:T(8,128)(2,1)S(1)} collective-permute-done((bf16[2048,64]{0,1:T(8,128)(2,1)S(1)}, bf16[2048,64]{0,1:T(8,128)(2,1)S(1)}, u32[]{:S(2)}, u32[]{:S(2)}) %collective-permute-start.7) | collective-permute-done | bytes 262176 | tf_op jit(solution)/shard_map/ppermute | solution.py:23
  91.5 0.0 collective-permute-start.8
  91.5 0.7 bitcast_dynamic-update-slice_fusion.7
  92.2 13.4 %collective-permute-done.8 = bf16[2048,64]{0,1:T(8,128)(2,1)S(1)} collective-permute-done((bf16[2048,64]{0,1:T(8,128)(2,1)S(1)}, bf16[2048,64]{0,1:T(8,128)(2,1)S(1)}, u32[]{:S(2)}, u32[]{:S(2)}) %collective-permute-start.8) | collective-permute-done | bytes 262176 | tf_op jit(solution)/shard_map/ppermute | solution.py:23
  105.6 0.0 collective-permute-start.9
  105.6 0.7 bitcast_dynamic-update-slice_fusion.6
  106.3 13.5 %collective-permute-done.9 = bf16[2048,64]{0,1:T(8,128)(2,1)S(1)} collective-permute-done((bf16[2048,64]{0,1:T(8,128)(2,1)S(1)}, bf16[2048,64]{0,1:T(8,128)(2,1)S(1)}, u32[]{:S(2)}, u32[]{:S(2)}) %collective-permute-start.9) | collective-permute-done | bytes 262176 | tf_op jit(solution)/shard_map/ppermute | solution.py:23
  119.8 0.0 collective-permute-start.10
  119.8 0.7 bitcast_dynamic-update-slice_fusion.5
  120.5 13.4 %collective-permute-done.10 = bf16[2048,64]{0,1:T(8,128)(2,1)S(1)} collective-permute-done((bf16[2048,64]{0,1:T(8,128)(2,1)S(1)}, bf16[2048,64]{0,1:T(8,128)(2,1)S(1)}, u32[]{:S(2)}, u32[]{:S(2)}) %collective-permute-start.10) | collective-permute-done | bytes 262176 | tf_op jit(solution)/shard_map/ppermute | solution.py:23
  133.9 0.0 collective-permute-start.11
  133.9 0.7 bitcast_dynamic-update-slice_fusion.4
  134.6 13.1 %collective-permute-done.11 = bf16[2048,64]{0,1:T(8,128)(2,1)S(1)} collective-permute-done((bf16[2048,64]{0,1:T(8,128)(2,1)S(1)}, bf16[2048,64]{0,1:T(8,128)(2,1)S(1)}, u32[]{:S(2)}, u32[]{:S(2)}) %collective-permute-start.11) | collective-permute-done | bytes 262176 | tf_op jit(solution)/shard_map/ppermute | solution.py:23
  147.7 0.0 collective-permute-start.12
  147.7 0.7 bitcast_dynamic-update-slice_fusion.3
  148.4 13.7 %collective-permute-done.12 = bf16[2048,64]{0,1:T(8,128)(2,1)S(1)} collective-permute-done((bf16[2048,64]{0,1:T(8,128)(2,1)S(1)}, bf16[2048,64]{0,1:T(8,128)(2,1)S(1)}, u32[]{:S(2)}, u32[]{:S(2)}) %collective-permute-start.12) | collective-permute-done | bytes 262176 | tf_op jit(solution)/shard_map/ppermute | solution.py:23
  162.2 0.0 collective-permute-start.13
  162.2 0.7 bitcast_dynamic-update-slice_fusion.2
  162.9 7.4 %collective-permute-done.13 = bf16[2048,64]{0,1:T(8,128)(2,1)S(1)} collective-permute-done((bf16[2048,64]{0,1:T(8,128)(2,1)S(1)}, bf16[2048,64]{0,1:T(8,128)(2,1)S(1)}, u32[]{:S(2)}, u32[]{:S(2)}) %collective-permute-start.13) | collective-permute-done | bytes 262176 | tf_op jit(solution)/shard_map/ppermute | solution.py:23
  170.3 0.0 collective-permute-start.14
  170.3 0.7 bitcast_dynamic-update-slice_fusion.1
  171.0 7.8 %collective-permute-done.14 = bf16[2048,64]{0,1:T(8,128)(2,1)S(1)} collective-permute-done((bf16[2048,64]{0,1:T(8,128)(2,1)S(1)}, bf16[2048,64]{0,1:T(8,128)(2,1)S(1)}, u32[]{:S(2)}, u32[]{:S(2)}) %collective-permute-start.14) | collective-permute-done | bytes 262176 | tf_op jit(solution)/shard_map/ppermute | solution.py:23
  178.8 0.7 bitcast_dynamic-update-slice_fusion
  179.5 5.1 %gather_fusion = bf16[16,2048,64]{1,2,0:T(8,128)(2,1)} fusion(bf16[16,2048,64]{1,2,0:T(8,128)(2,1)} %bitcast_dynamic-update-slice_fusion, s32[1024]{0:T(1024)S(1)} %pad_clamp_fusion), kind=kCustom, calls=%fused_computation | custom fusion | bytes 8388672 | tf_op jit(solution)/shard_map/gather | solution.py:25
  184.6 8.2 %fusion.18 = bf16[128,2048]{1,0:T(8,128)(2,1)S(1)} fusion(bf16[128,4096]{1,0:T(8,128)(2,1)S(1)} %copy-done.1, bf16[4096,2048]{1,0:T(8,128)(2,1)} %all-gather.3.cloned.1.call-done, bf16[128]{0:T(256)(128)(2,1)S(1)} %fusion.38), kind=kOutput, calls=%fused_computation.32 | convolution fusion | flops 2148007936 | bytes 18350336 | tf_op jit(solution)/shard_map/dot_general | solution.py:56
  192.7 9.9 %fusion.37 = f32[1024,2048]{1,0:T(8,128)} fusion(bf16[128,2048]{1,0:T(8,128)(2,1)S(1)} %fusion.18, bf16[2048,1024]{0,1:T(8,128)(2,1)} %bitcast.54, bf16[128,2048]{1,0:T(8,128)(2,1)} %param.10), kind=kOutput, calls=%fused_computation.40 | convolution fusion | flops 1073872896 | bytes 13631488 | tf_op jit(solution)/shard_map/dot_general | solution.py:68
  202.6 194.6 %all-reduce.2 = (bf16[1024,2048]{1,0:T(8,128)(2,1)}, f32[]{:T(128)}) all-reduce(f32[1024,2048]{1,0:T(8,128)} %fusion.37, f32[]{:T(128)} %convert_reduce_fusion), channel_id=1, replica_groups=mesh['groups'=2,'wide'=16] {'wide'}, use_global_device_ids=true, to_apply=%region_0.1 | all-reduce | flops 2097153 | bytes 12582920 | tf_op jit(solution)/shard_map/psum | solution.py:71
  397.9 0.7 fusion.41
  398.6 6.9 %fusion.19 = f32[384]{0:T(512)S(1)} fusion(bf16[1024,384]{1,0:T(8,128)(2,1)S(1)} %copy-done.4, bf16[2048,384]{1,0:T(8,128)(2,1)S(1)} %copy-done, bf16[1024,2048]{1,0:T(8,128)(2,1)} %get-tuple-element.5, bf16[1024,2048]{1,0:T(8,128)(2,1)} %all-gather.5.cloned.1.call-done, f32[]{:T(128)} %bitcast.19), kind=kOutput, calls=%fused_computation.33 | convolution fusion | flops 1622277760 | bytes 10749444 | tf_op jit(solution)/shard_map/dot_general | solution.py:36
  405.5 3.0 fusion.20
  408.5 2.9 fusion.21
  411.4 3.0 fusion.22
  414.5 3.3 fusion.23
  417.7 2.9 fusion.24
  421.3 0.6 multiply_multiply_fusion
  (25 shorter events, 0.1 us)
Async XLA Ops:
  6.5 392.0 %copy-start = (bf16[2048,384]{1,0:T(8,128)(2,1)S(1)}, bf16[2048,384]{1,0:T(8,128)(2,1)}, u32[]{:S(2)}) copy-start(bf16[2048,384]{1,0:T(8,128)(2,1)} %param.18) | copy-start | bytes 4718596
  6.5 178.0 %all-gather.3.cloned.1.call-start = ((), (), s32[]{:S(2)}) async-start(), calls=%async_computation | async-start | bytes 17825792 | tf_op jit(solution)/shard_map/all_gather | solution.py:58
  7.3 391.3 %all-gather.5.cloned.1.call-start = ((), (), s32[]{:S(2)}) async-start(), calls=%async_computation.1 | async-start | bytes 4456448 | tf_op jit(solution)/shard_map/all_gather | solution.py:74
  7.3 7.5 %collective-permute-start = (bf16[2048,64]{0,1:T(8,128)(2,1)}, bf16[2048,64]{0,1:T(8,128)(2,1)S(1)}, u32[]{:S(2)}, u32[]{:S(2)}) collective-permute-start(bf16[2048,64]{0,1:T(8,128)(2,1)} %param.13), channel_id=1, source_target_pairs={{0,1},{1,2},{2,3},{3,4},{4,5},{5,6},{6,7},{7,8},{8,9},{9,10},{10,1... | collective-permute-start | bytes 786440 | tf_op jit(solution)/shard_map/ppermute | solution.py:23
  14.8 4.5 %collective-permute-start.1 = (bf16[2048,64]{0,1:T(8,128)(2,1)S(1)}, bf16[2048,64]{0,1:T(8,128)(2,1)S(1)}, u32[]{:S(2)}, u32[]{:S(2)}) collective-permute-start(bf16[2048,64]{0,1:T(8,128)(2,1)S(1)} %collective-permute-done), channel_id=1, source_target_pairs={{0,1},{1,2},{2,3},{3,4},{4,5},{5,6},{6,7},{7,8},{8,9},{9,10},{10,1... | collective-permute-start | bytes 786440 | tf_op jit(solution)/shard_map/ppermute | solution.py:23
  19.3 11.3 %collective-permute-start.2 = (bf16[2048,64]{0,1:T(8,128)(2,1)S(1)}, bf16[2048,64]{0,1:T(8,128)(2,1)S(1)}, u32[]{:S(2)}, u32[]{:S(2)}) collective-permute-start(bf16[2048,64]{0,1:T(8,128)(2,1)S(1)} %collective-permute-done.1), channel_id=1, source_target_pairs={{0,1},{1,2},{2,3},{3,4},{4,5},{5,6},{6,7},{7,8},{8,9},{9,10},{10,1... | collective-permute-start | bytes 786440 | tf_op jit(solution)/shard_map/ppermute | solution.py:23
  30.6 10.3 %collective-permute-start.3 = (bf16[2048,64]{0,1:T(8,128)(2,1)S(1)}, bf16[2048,64]{0,1:T(8,128)(2,1)S(1)}, u32[]{:S(2)}, u32[]{:S(2)}) collective-permute-start(bf16[2048,64]{0,1:T(8,128)(2,1)S(1)} %collective-permute-done.2), channel_id=1, source_target_pairs={{0,1},{1,2},{2,3},{3,4},{4,5},{5,6},{6,7},{7,8},{8,9},{9,10},{10,1... | collective-permute-start | bytes 786440 | tf_op jit(solution)/shard_map/ppermute | solution.py:23
  40.9 14.1 %collective-permute-start.4 = (bf16[2048,64]{0,1:T(8,128)(2,1)S(1)}, bf16[2048,64]{0,1:T(8,128)(2,1)S(1)}, u32[]{:S(2)}, u32[]{:S(2)}) collective-permute-start(bf16[2048,64]{0,1:T(8,128)(2,1)S(1)} %collective-permute-done.3), channel_id=1, source_target_pairs={{0,1},{1,2},{2,3},{3,4},{4,5},{5,6},{6,7},{7,8},{8,9},{9,10},{10,1... | collective-permute-start | bytes 786440 | tf_op jit(solution)/shard_map/ppermute | solution.py:23
  55.0 13.8 %collective-permute-start.5 = (bf16[2048,64]{0,1:T(8,128)(2,1)S(1)}, bf16[2048,64]{0,1:T(8,128)(2,1)S(1)}, u32[]{:S(2)}, u32[]{:S(2)}) collective-permute-start(bf16[2048,64]{0,1:T(8,128)(2,1)S(1)} %collective-permute-done.4), channel_id=1, source_target_pairs={{0,1},{1,2},{2,3},{3,4},{4,5},{5,6},{6,7},{7,8},{8,9},{9,10},{10,1... | collective-permute-start | bytes 786440 | tf_op jit(solution)/shard_map/ppermute | solution.py:23
  68.8 8.9 %collective-permute-start.6 = (bf16[2048,64]{0,1:T(8,128)(2,1)S(1)}, bf16[2048,64]{0,1:T(8,128)(2,1)S(1)}, u32[]{:S(2)}, u32[]{:S(2)}) collective-permute-start(bf16[2048,64]{0,1:T(8,128)(2,1)S(1)} %collective-permute-done.5), channel_id=1, source_target_pairs={{0,1},{1,2},{2,3},{3,4},{4,5},{5,6},{6,7},{7,8},{8,9},{9,10},{10,1... | collective-permute-start | bytes 786440 | tf_op jit(solution)/shard_map/ppermute | solution.py:23
  77.7 13.8 %collective-permute-start.7 = (bf16[2048,64]{0,1:T(8,128)(2,1)S(1)}, bf16[2048,64]{0,1:T(8,128)(2,1)S(1)}, u32[]{:S(2)}, u32[]{:S(2)}) collective-permute-start(bf16[2048,64]{0,1:T(8,128)(2,1)S(1)} %collective-permute-done.6), channel_id=1, source_target_pairs={{0,1},{1,2},{2,3},{3,4},{4,5},{5,6},{6,7},{7,8},{8,9},{9,10},{10,1... | collective-permute-start | bytes 786440 | tf_op jit(solution)/shard_map/ppermute | solution.py:23
  91.5 14.1 %collective-permute-start.8 = (bf16[2048,64]{0,1:T(8,128)(2,1)S(1)}, bf16[2048,64]{0,1:T(8,128)(2,1)S(1)}, u32[]{:S(2)}, u32[]{:S(2)}) collective-permute-start(bf16[2048,64]{0,1:T(8,128)(2,1)S(1)} %collective-permute-done.7), channel_id=1, source_target_pairs={{0,1},{1,2},{2,3},{3,4},{4,5},{5,6},{6,7},{7,8},{8,9},{9,10},{10,1... | collective-permute-start | bytes 786440 | tf_op jit(solution)/shard_map/ppermute | solution.py:23
  105.6 14.2 %collective-permute-start.9 = (bf16[2048,64]{0,1:T(8,128)(2,1)S(1)}, bf16[2048,64]{0,1:T(8,128)(2,1)S(1)}, u32[]{:S(2)}, u32[]{:S(2)}) collective-permute-start(bf16[2048,64]{0,1:T(8,128)(2,1)S(1)} %collective-permute-done.8), channel_id=1, source_target_pairs={{0,1},{1,2},{2,3},{3,4},{4,5},{5,6},{6,7},{7,8},{8,9},{9,10},{10,1... | collective-permute-start | bytes 786440 | tf_op jit(solution)/shard_map/ppermute | solution.py:23
  119.8 14.1 %collective-permute-start.10 = (bf16[2048,64]{0,1:T(8,128)(2,1)S(1)}, bf16[2048,64]{0,1:T(8,128)(2,1)S(1)}, u32[]{:S(2)}, u32[]{:S(2)}) collective-permute-start(bf16[2048,64]{0,1:T(8,128)(2,1)S(1)} %collective-permute-done.9), channel_id=1, source_target_pairs={{0,1},{1,2},{2,3},{3,4},{4,5},{5,6},{6,7},{7,8},{8,9},{9,10},{10,1... | collective-permute-start | bytes 786440 | tf_op jit(solution)/shard_map/ppermute | solution.py:23
  133.9 13.8 %collective-permute-start.11 = (bf16[2048,64]{0,1:T(8,128)(2,1)S(1)}, bf16[2048,64]{0,1:T(8,128)(2,1)S(1)}, u32[]{:S(2)}, u32[]{:S(2)}) collective-permute-start(bf16[2048,64]{0,1:T(8,128)(2,1)S(1)} %collective-permute-done.10), channel_id=1, source_target_pairs={{0,1},{1,2},{2,3},{3,4},{4,5},{5,6},{6,7},{7,8},{8,9},{9,10},{10,1... | collective-permute-start | bytes 786440 | tf_op jit(solution)/shard_map/ppermute | solution.py:23
  147.7 14.5 %collective-permute-start.12 = (bf16[2048,64]{0,1:T(8,128)(2,1)S(1)}, bf16[2048,64]{0,1:T(8,128)(2,1)S(1)}, u32[]{:S(2)}, u32[]{:S(2)}) collective-permute-start(bf16[2048,64]{0,1:T(8,128)(2,1)S(1)} %collective-permute-done.11), channel_id=1, source_target_pairs={{0,1},{1,2},{2,3},{3,4},{4,5},{5,6},{6,7},{7,8},{8,9},{9,10},{10,1... | collective-permute-start | bytes 786440 | tf_op jit(solution)/shard_map/ppermute | solution.py:23
  162.2 8.1 %collective-permute-start.13 = (bf16[2048,64]{0,1:T(8,128)(2,1)S(1)}, bf16[2048,64]{0,1:T(8,128)(2,1)S(1)}, u32[]{:S(2)}, u32[]{:S(2)}) collective-permute-start(bf16[2048,64]{0,1:T(8,128)(2,1)S(1)} %collective-permute-done.12), channel_id=1, source_target_pairs={{0,1},{1,2},{2,3},{3,4},{4,5},{5,6},{6,7},{7,8},{8,9},{9,10},{10,1... | collective-permute-start | bytes 786440 | tf_op jit(solution)/shard_map/ppermute | solution.py:23
  170.3 8.5 %collective-permute-start.14 = (bf16[2048,64]{0,1:T(8,128)(2,1)S(1)}, bf16[2048,64]{0,1:T(8,128)(2,1)S(1)}, u32[]{:S(2)}, u32[]{:S(2)}) collective-permute-start(bf16[2048,64]{0,1:T(8,128)(2,1)S(1)} %collective-permute-done.13), channel_id=1, source_target_pairs={{0,1},{1,2},{2,3},{3,4},{4,5},{5,6},{6,7},{7,8},{8,9},{9,10},{10,1... | collective-permute-start | bytes 786440 | tf_op jit(solution)/shard_map/ppermute | solution.py:23
  179.5 5.1 %copy-start.1 = (bf16[128,4096]{1,0:T(8,128)(2,1)S(1)}, bf16[128,4096]{1,0:T(8,128)(2,1)}, u32[]{:S(2)}) copy-start(bf16[128,4096]{1,0:T(8,128)(2,1)} %param.11) | copy-start | bytes 3145732
  202.6 195.3 %copy-start.5 = (s32[6]{0:T(128)S(1)}, s32[6]{0:T(128)}, u32[]{:S(2)}) copy-start(s32[6]{0:T(128)} %param.16) | copy-start | bytes 76
  202.6 196.0 %copy-start.4 = (bf16[1024,384]{1,0:T(8,128)(2,1)S(1)}, bf16[1024,384]{1,0:T(8,128)(2,1)}, u32[]{:S(2)}) copy-start(bf16[1024,384]{1,0:T(8,128)(2,1)} %param.17) | copy-start | bytes 2359300
  398.6 6.9 %copy-start.2 = (bf16[1024,2048]{1,0:T(8,128)(2,1)S(1)}, bf16[1024,2048]{1,0:T(8,128)(2,1)}, u32[]{:S(2)}) copy-start(bf16[1024,2048]{1,0:T(8,128)(2,1)} %all-gather.5.cloned.1.call-done) | copy-start | bytes 12582916
  398.6 6.9 %copy-start.3 = (bf16[1024,2048]{1,0:T(8,128)(2,1)S(1)}, bf16[1024,2048]{1,0:T(8,128)(2,1)}, u32[]{:S(2)}) copy-start(bf16[1024,2048]{1,0:T(8,128)(2,1)} %get-tuple-element.5) | copy-start | bytes 12582916
Sparse Core Ops, SparseCore 0:
  9.5 154.9 all-gather.2
  166.7 59.6 all-gather.4
